TPU v7x, 128 devices: a whole 4x4x4 slice. The times are simulated.
128 devices in a mesh: dp: 4 (over z_lo, core), tensor: 32 (over y, x, z_hi).
Axes of the slice: x: 4, y: 4, z: 4 (z_hi: 2, z_lo: 2; z = z_hi * 2 + z_lo), core: 2. Of those that a mesh axis runs over, the one named last changes fastest.
Arguments:
- stream: bfloat16 [6144, 2560], P(('dp', 'tensor')), may hold values from -26 to 26
- lengths: int32 [4, 6], P('dp'), may hold values from 16 to 768, as said below
- page_table: int32 [384], P('dp'), may hold values from 0 to 383, as said below
- request_prompt: int32 [64], P('dp'), may hold values from 0 to 23
- attn_gain: bfloat16 [2560], replicated, may hold values from 0.099609375 to 1.8984375
- query_gain: bfloat16 [128], replicated, may hold values from 0.5 to 10, as said below
- key_gain: bfloat16 [128], replicated, may hold values from 0.5 to 10, as said below
- mlp_gain: bfloat16 [2560], replicated, may hold values from 0.099609375 to 1.8984375
- w_query: bfloat16 [2560, 4096], P(None, 'tensor'), may hold values from -0.125 to 0.125
- key_value_weight: bfloat16 [2560, 2048], P(None, 'tensor'), may hold values from -0.125 to 0.125
- w_out: bfloat16 [4096, 2560], P('tensor'), may hold values from -0.5 to 0.5
- w_gate: bfloat16 [2560, 9728], P(None, 'tensor'), may hold values from -0.125 to 0.125
- w_up: bfloat16 [2560, 9728], P(None, 'tensor'), may hold values from -0.125 to 0.125
- w_down: bfloat16 [9728, 2560], P('tensor'), may hold values from -0.0625 to 0.0625
Outputs:
- layer_out: bfloat16 [6144, 2560], P(('dp', 'tensor'))
- paged_key_value_cache: bfloat16 [384, 16, 2048], P('dp', None, 'tensor')
- request_state: bfloat16 [64, 2560], P('dp', 'tensor')
Inputs may be any that keep to these rules, and one draw needn't show every extreme that they name: Every length is a multiple of 16; each batch's lengths add up to 1536, and the largest length of each batch is exactly 768. page_table is a permutation of all global slots; slot v belongs to owner v // 96, and each batch writes exactly 24 pages to each owner. `query_gain`: positive gains. `key_gain`: positive gains.
All inputs are finite; a program needn't handle non-finite values.
Results may differ from a plain program's by a relative error of at most 0.02.
The roundings to bfloat16 on the way count: a program that leaves them out, or rounds other values in their place, can miss the bound.
Values may be sent and summed in bfloat16 or wider, within the bound.
No kernel may reach another device: no remote copies, remote signals or barrier semaphores. Data moves between devices by JAX's collectives and lax.ppermute only.
A program may use at most 128 MiB of HBM per device.

v0:
```python
import math
import jax
import jax.numpy as jnp
from jax import lax
from jax.sharding import PartitionSpec as P

KEY_VALUE_HEADS = 8
HEAD_SIZE = 128
PAGE_TOKENS = 16
TENSOR = ("ty", "tx", "tz")
TENSOR_SHAPE = (4, 4, 2)
epsilon = 1e-06
rope_base = 1000000.0


def partner_2(value, axis, bit):
    mask = 2**bit
    pairs = [(source, source ^ mask) for source in range(lax.axis_size(axis))]
    return lax.ppermute(value, axis, pairs)


def scatter_sum(partial, parts):
    pieces = partial.reshape((parts, partial.shape[0] // parts) + partial.shape[1:])
    got = lax.all_to_all(pieces, TENSOR, 0, 0, tiled=True)
    return jnp.sum(got.astype(jnp.float32), axis=0)


def gather_rows(rows):
    rows = lax.all_gather(rows, "tz", axis=0, tiled=True)
    return lax.all_gather(rows, ("ty", "tx"), axis=0, tiled=True)


def row_norm(inputs, gain):
    inputs = inputs.astype(jnp.float32)
    scale = lax.rsqrt(jnp.mean(inputs * inputs, axis=-1, keepdims=True) + epsilon)
    return inputs * scale * gain.astype(jnp.float32)


def rotate(inputs, position):
    half_dim = inputs.shape[-1] // 2
    frequency = rope_base ** (-2.0 * jnp.arange(half_dim, dtype=jnp.float32) / inputs.shape[-1])
    angles = position.astype(jnp.float32)[:, None] * frequency[None, :]
    cosine = jnp.cos(angles)[:, None, :]
    sine_part = jnp.sin(angles)[:, None, :]
    front = inputs[..., :half_dim]
    second = inputs[..., half_dim:]
    return jnp.concatenate(
        [front * cosine - second * sine_part, second * cosine + front * sine_part], axis=-1
    )


def prompt_layout(lengths_row, token_count):
    prompt_ends = jnp.cumsum(lengths_row)
    prompt_starts = prompt_ends - lengths_row
    row_ids = jnp.arange(token_count, dtype=jnp.int32)
    prompt = jnp.sum((row_ids[:, None] >= prompt_ends[None, :]).astype(jnp.int32), axis=1)
    inside = (row_ids[:, None] >= prompt_starts[None, :]) & (
        row_ids[:, None] < prompt_ends[None, :]
    )
    offset = jnp.sum(jnp.where(inside, prompt_starts[None, :], 0), axis=1)
    return (prompt, row_ids - offset, prompt_starts, prompt_ends)


def per_device(
    stream,
    lengths,
    page_table,
    request_prompt,
    attn_gain,
    query_gain,
    key_gain,
    mlp_gain,
    w_query,
    key_value_weight,
    w_out,
    w_gate,
    w_up,
    w_down,
):
    tok_dev = stream.shape[0]
    tensor_element_count = lax.axis_size(TENSOR)
    token_count = tok_dev * tensor_element_count
    my_index = lax.axis_index(TENSOR)
    heads_dev = w_query.shape[1] // HEAD_SIZE
    query_cols = heads_dev * HEAD_SIZE
    prompt, position, prompt_starts, prompt_ends = prompt_layout(lengths[0], token_count)
    portion = gather_rows(row_norm(stream, attn_gain).astype(jnp.bfloat16))
    key_value_group = tensor_element_count // KEY_VALUE_HEADS
    head_weight = key_value_weight
    for bit_id in range(key_value_group.bit_length() - 1):
        partner = partner_2(head_weight, TENSOR, bit_id)
        upper_half = my_index // 2**bit_id % 2
        head_weight = jnp.where(
            upper_half == 1,
            jnp.concatenate([partner, head_weight], axis=1),
            jnp.concatenate([head_weight, partner], axis=1),
        )
    joined = jnp.dot(
        portion, jnp.concatenate([w_query, head_weight], axis=1), preferred_element_type=jnp.float32
    )
    queries = joined[:, :query_cols].reshape(token_count, heads_dev, HEAD_SIZE)
    kv_part = joined[:, query_cols:].astype(jnp.bfloat16)
    key_flat = rotate(row_norm(kv_part[:, None, :HEAD_SIZE], key_gain), position).astype(
        jnp.bfloat16
    )[:, 0, :]
    value_matrix_rows = kv_part[:, HEAD_SIZE:]
    q_rot = rotate(row_norm(queries, query_gain), position).astype(jnp.bfloat16)
    piece_cols = key_value_weight.shape[1]
    head_rows = jnp.concatenate([key_flat, value_matrix_rows], axis=1)
    own_cols = lax.dynamic_slice_in_dim(
        head_rows, my_index % key_value_group * piece_cols, piece_cols, 1
    )
    page_count = token_count // PAGE_TOKENS
    page_rows = own_cols.reshape(page_count, PAGE_TOKENS, piece_cols)
    group_count = lax.axis_size("dp")
    capacity = page_count // group_count
    owners = page_table // page_count
    slot_ids = page_table % page_count
    hits = (owners[:, None] == jnp.arange(group_count, dtype=jnp.int32)[None, :]).astype(jnp.int32)
    order_in = jnp.sum((jnp.cumsum(hits, axis=0) - hits) * hits, axis=1)
    buffer_pos = owners * capacity + order_in
    source = (
        jnp.zeros((page_count,), jnp.int32)
        .at[buffer_pos]
        .set(jnp.arange(page_count, dtype=jnp.int32))
    )
    send_pages = page_rows[source].reshape(group_count, capacity, PAGE_TOKENS, piece_cols)
    send_slots = slot_ids[source].reshape(group_count, capacity)
    got_pages, got_slots = (
        lax.all_to_all(send_pages, "dp", split_axis=0, concat_axis=0, tiled=True),
        lax.all_to_all(send_slots, "dp", split_axis=0, concat_axis=0, tiled=True),
    )
    paged_key_value_cache = (
        jnp.zeros((page_count, PAGE_TOKENS, piece_cols), jnp.bfloat16)
        .at[got_slots.reshape(-1)]
        .set(got_pages.reshape(page_count, PAGE_TOKENS, piece_cols))
    )
    block_rows = min(512, token_count)
    block_total = token_count // block_rows
    score_scale = math.sqrt(HEAD_SIZE)
    all_ids = jnp.arange(token_count, dtype=jnp.int32)
    local_ids = jnp.arange(block_rows, dtype=jnp.int32)

    def dense_block(block_index):
        first_row = block_index * block_rows
        key_count = first_row + block_rows
        key_first = max(0, first_row - 768)
        q_block = q_rot[first_row:key_count]
        q_prompt = prompt[first_row:key_count]
        row_ids = first_row + local_ids
        scores = (
            jnp.einsum(
                "qhd,kd->hqk",
                q_block,
                key_flat[key_first:key_count],
                preferred_element_type=jnp.float32,
            )
            / score_scale
        )
        allowed = (
            (q_prompt[:, None] == prompt[None, key_first:key_count])
            & (row_ids[:, None] >= all_ids[None, key_first:key_count])
        )[None]
        peak = jnp.max(jnp.where(allowed, scores, -jnp.inf), axis=2, keepdims=True)
        weight = jnp.where(allowed, jnp.exp(scores - peak), 0.0)
        total_weight = jnp.sum(weight, axis=2, keepdims=True)
        running = jnp.einsum(
            "hqk,kd->hqd",
            weight.astype(jnp.bfloat16),
            value_matrix_rows[key_first:key_count],
            preferred_element_type=jnp.float32,
        )
        return (running / total_weight).astype(jnp.bfloat16)

    blocks_out = jnp.stack([dense_block(block_index) for block_index in range(block_total)])
    attn = jnp.transpose(blocks_out, (0, 2, 1, 3)).reshape(token_count, query_cols)
    attn_sum = scatter_sum(
        jnp.dot(attn, w_out, preferred_element_type=jnp.float32).astype(jnp.bfloat16),
        tensor_element_count,
    )
    resid = (stream.astype(jnp.float32) + attn_sum).astype(jnp.bfloat16)
    portion = gather_rows(row_norm(resid, mlp_gain).astype(jnp.bfloat16))
    paged_key_value_cache, portion = lax.optimization_barrier((paged_key_value_cache, portion))
    both = jnp.dot(
        portion, jnp.concatenate([w_gate, w_up], axis=1), preferred_element_type=jnp.float32
    )
    gate_rows = both[:, : w_gate.shape[1]]
    upward = both[:, w_gate.shape[1] :]
    hidden = (jax.nn.silu(gate_rows) * upward).astype(jnp.bfloat16)
    width = w_down.shape[1]
    feat = width // tensor_element_count
    nprompt = prompt_ends.shape[0]
    end_pick = ((prompt_ends - 1)[:, None] == all_ids[None, :]).astype(jnp.bfloat16)
    end_hidden = jnp.dot(end_pick, hidden, preferred_element_type=jnp.float32).astype(jnp.bfloat16)
    end_down = jnp.dot(end_hidden, w_down, preferred_element_type=jnp.float32).astype(jnp.bfloat16)
    my_rows = my_index * tok_dev + jnp.arange(tok_dev, dtype=jnp.int32)
    select = ((prompt_ends - 1)[:, None] == my_rows[None, :]).astype(jnp.bfloat16)
    end_resid = jnp.dot(select, resid, preferred_element_type=jnp.float32).astype(jnp.bfloat16)

    def by_feature_block(rows):
        blocks = rows.reshape(nprompt, tensor_element_count, feat)
        return jnp.transpose(blocks, (1, 0, 2)).reshape(tensor_element_count, nprompt * feat)

    extra = jnp.concatenate([by_feature_block(end_down), by_feature_block(end_resid)], axis=1)
    extra_cols = 128
    extra = jnp.pad(extra, ((0, 0), (0, tok_dev * extra_cols - extra.shape[1])))
    wide_weight = jnp.concatenate(
        [w_down, jnp.zeros((w_down.shape[0], extra_cols), w_down.dtype)], axis=1
    )
    down = jnp.dot(hidden, wide_weight, preferred_element_type=jnp.float32).astype(jnp.bfloat16)
    payload = lax.dynamic_update_slice(
        down.reshape(tensor_element_count, tok_dev, width + extra_cols),
        extra.reshape(tensor_element_count, tok_dev, extra_cols),
        (0, 0, width),
    )
    got = lax.all_to_all(payload, TENSOR, 0, 0, tiled=True)
    summed = jnp.sum(got.astype(jnp.float32), axis=0)
    mlp_sum = summed[:, :width]
    layer_out = (resid.astype(jnp.float32) + mlp_sum).astype(jnp.bfloat16)
    tail = summed[:, width:].reshape(-1)
    end_rows = (
        (tail[: nprompt * feat] + tail[nprompt * feat : 2 * nprompt * feat])
        .reshape(nprompt, feat)
        .astype(jnp.bfloat16)
    )
    table = lax.all_gather(end_rows, "dp", axis=0, tiled=True)
    pick = (request_prompt[:, None] == jnp.arange(table.shape[0], dtype=jnp.int32)[None, :]).astype(
        jnp.bfloat16
    )
    request_state = jnp.dot(pick, table, preferred_element_type=jnp.float32).astype(jnp.bfloat16)
    return (layer_out, paged_key_value_cache, request_state)


def solution(mesh):
    placed = (
        P(("dp",) + TENSOR, None),
        P("dp", None),
        P("dp"),
        P("dp"),
        P(),
        P(),
        P(),
        P(),
        P(None, TENSOR),
        P(None, TENSOR),
        P(TENSOR, None),
        P(None, TENSOR),
        P(None, TENSOR),
        P(TENSOR, None),
    )
    dp_size = mesh.shape["dp"]
    fine = jax.sharding.Mesh(mesh.devices.reshape((dp_size,) + TENSOR_SHAPE), ("dp",) + TENSOR)
    return jax.shard_map(
        per_device,
        mesh=fine,
        in_specs=placed,
        out_specs=(P(("dp",) + TENSOR, None), P("dp", None, TENSOR), P("dp", TENSOR)),
        check_vma=False,
    )
```

profile of v0, /device:TPU:27, one launch (start us, length us, event | category | flops | bytes accessed | tf_op | source)
XLA Modules:
  0.0 503.4 jit_solution(10188079126482272437)
XLA Ops:
  7.3 1.2 fusion.62
  8.5 0.7 convert_element_type.131
  9.2 1.1 fusion.64
  10.3 10.0 %all_gather.15 = bf16[96,2560]{1,0:T(8,128)(2,1)} all-gather(bf16[48,2560]{1,0:T(8,128)(2,1)S(1)} %fusion.64), channel_id=1, replica_groups=mesh['dp'=4,'ty'=4,'tx'=4,'tz'=2] {'tz'}, dimensions={0}, use_global_device_ids=true | all-gather | bytes 737280 | tf_op jit(solution)/shard_map/all_gather | solution.py:29
  20.3 2.8 collective-permute-start
  23.1 0.8 reduce-window.4
  23.9 0.7 fusion.114
  24.8 1.1 copy.29
  25.9 4.2 collective-permute-done
  30.2 0.3 collective-permute-start.1
  30.6 22.5 %collective-permute-done.1 = bf16[2560,128]{0,1:T(8,128)(2,1)S(1)} collective-permute-done((bf16[2560,128]{0,1:T(8,128)(2,1)S(1)}, bf16[2560,128]{0,1:T(8,128)(2,1)S(1)}, u32[]{:S(2)}, u32[]{:S(2)}) %collective-permute-start.1) | collective-permute-done | bytes 655392 | tf_op jit(solution)/shard_map/ppermute | solution.py:19
  53.1 0.3 maximum_select_fusion
  53.4 41.0 %all-gather.4.cloned.1.call-done = bf16[1536,2560]{1,0:T(8,128)(2,1)} async-done(((bf16[96,2560]{1,0:T(8,128)(2,1)}), bf16[1536,2560]{1,0:T(8,128)(2,1)}) %all-gather.4.cloned.1.call-update) | async-done | bytes 7864336 | tf_op jit(solution)/shard_map/all_gather | solution.py:30
  94.4 5.7 %fusion.129 = (bf16[1536,384]{0,1:T(8,128)(2,1)S(1)}, f32[1536,384]{0,1:T(8,128)S(1)}) fusion(bf16[1536,2560]{1,0:T(8,128)(2,1)} %all-gather.4.cloned.1.call-done, bf16[2560,256]{0,1:T(8,128)(2,1)S(1)} %maximum_select_fusion, bf16[2560,128]{0,1:T(8,128)(2,1)} %copy.29), kind=kOutput, calls=%fused_computation.201 | convolution fusion | flops 3024420864 | bytes 13369344 | tf_op jit(solution)/shard_map/dot_general | solution.py:98
  100.1 0.2 fusion.40
  100.3 0.1 multiply_bitcast_fusion
  100.5 0.1 fusion.42
  100.6 1.7 fusion.75
  102.4 0.4 select_reduce_fusion.1
  102.8 0.3 fusion.45
  103.1 0.6 fusion.24
  103.7 0.6 fusion.5
  104.4 0.9 fusion.20
  105.3 0.9 fusion.25
  106.2 0.7 select_reduce_fusion
  106.9 1.0 fusion.13
  107.9 1.1 fusion.32
  109.1 5.4 %convolution_convert_fusion.1 = bf16[1536,2560]{1,0:T(8,128)(2,1)} fusion(bf16[1536,128]{1,0:T(8,128)(2,1)S(1)} %bitcast.125, bf16[128,2560]{1,0:T(8,128)(2,1)S(1)} %copy-done), kind=kOutput, calls=%fused_computation.7 | convolution fusion | flops 1010565120 | bytes 8912896 | tf_op jit(solution)/shard_map/dot_general | solution.py:178
  114.4 9.3 %all-to-all-start = ((bf16[32,48,2560]{2,1,0:T(8,128)(2,1)}), bf16[32,48,2560]{2,1,0:T(8,128)(2,1)}, u32[]{:S(2)}, u32[]{:S(2)}) async-start(bf16[32,48,2560]{2,1,0:T(8,128)(2,1)} %bitcast.123), calls=%async_computation | async-start | bytes 15728640 | tf_op jit(solution)/shard_map/all_to_all | solution.py:24
  123.8 121.6 %all-to-all-done = bf16[32,48,2560]{2,1,0:T(8,128)(2,1)} async-done(((bf16[32,48,2560]{2,1,0:T(8,128)(2,1)}), bf16[32,48,2560]{2,1,0:T(8,128)(2,1)}, u32[]{:S(2)}, u32[]{:S(2)}) %all-to-all-start) | async-done | bytes 7864352 | tf_op jit(solution)/shard_map/all_to_all | solution.py:24
  245.4 4.5 convert_reduce_fusion.1
  250.0 0.2 fusion.66
  250.3 8.2 %all_gather.17 = bf16[96,2560]{1,0:T(8,128)(2,1)} all-gather(bf16[48,2560]{1,0:T(8,128)(2,1)S(1)} %fusion.68), channel_id=1, replica_groups=mesh['dp'=4,'ty'=4,'tx'=4,'tz'=2] {'tz'}, dimensions={0}, use_global_device_ids=true | all-gather | bytes 737280 | tf_op jit(solution)/shard_map/all_gather | solution.py:29
  258.8 0.2 select_reduce_fusion.2
  259.0 0.9 scatter_custom_fusion
  259.9 1.2 gather_fusion
  261.1 0.7 all_to_all.16
  261.8 5.6 %all-to-all-start.1 = ((s32[4,1,24]{2,1,0:T(1,128)}), s32[4,1,24]{2,1,0:T(1,128)S(1)}, u32[]{:S(2)}, u32[]{:S(2)}) async-start(s32[4,1,24]{2,1,0:T(1,128)} %bitcast.29), calls=%async_computation.1 | async-start | bytes 4096 | tf_op jit(solution)/shard_map/all_to_all | solution.py:131
  267.4 3.0 all-to-all-done.1
  270.4 0.5 broadcast.485
  271.0 0.7 reduce.13
  271.7 0.2 fusion.90
  271.9 0.2 copy.31
  272.1 0.7 gather_fusion.1
  272.8 1.0 reshape.716
  273.8 4.0 all-to-all-start.2
  277.8 4.5 all-to-all-done.2
  282.3 0.3 reshape.717
  282.7 3.5 scatter_fusion
  286.1 0.2 convolution_convert_fusion.2
  286.6 39.5 %all-gather.6.cloned.1.call-done = bf16[1536,2560]{1,0:T(8,128)(2,1)} async-done(((bf16[96,2560]{1,0:T(8,128)(2,1)}), bf16[1536,2560]{1,0:T(8,128)(2,1)}) %all-gather.6.cloned.1.call-update) | async-done | bytes 7864336 | tf_op jit(solution)/shard_map/all_gather | solution.py:30
  326.2 7.8 %fusion.1 = f32[1536,608]{0,1:T(8,128)S(1)} fusion(bf16[1536,2560]{1,0:T(8,128)(2,1)} %all-gather.6.cloned.1.call-done, bf16[2560,304]{0,1:T(8,128)(2,1)S(1)} %copy-done.7, bf16[2560,304]{0,1:T(8,128)(2,1)} %param.25), kind=kOutput, calls=%fused_computation.12 | convolution fusion | flops 4787732480 | bytes 14712832 | tf_op jit(solution)/shard_map/dot_general | solution.py:184
  334.0 0.6 fusion.12
  334.6 0.8 copy-done.3
  335.4 1.0 convolution_convert_fusion.3
  336.3 6.8 %convolution_convert_fusion = bf16[1536,2688]{1,0:T(8,128)(2,1)} fusion(bf16[1536,304]{0,1:T(8,128)(2,1)S(1)} %fusion.12, bf16[304,2560]{1,0:T(8,128)(2,1)S(1)} %copy-done.3), kind=kOutput, calls=%fused_computation.6 | convolution fusion | flops 2514419712 | bytes 10747904 | tf_op jit(solution)/shard_map/dot_general | solution.py:210
  343.6 0.8 constant_dynamic-update-slice_fusion
  344.4 9.2 %all-to-all-start.3 = ((bf16[32,48,2688]{2,1,0:T(8,128)(2,1)}), bf16[32,48,2688]{2,1,0:T(8,128)(2,1)}, u32[]{:S(2)}, u32[]{:S(2)}) async-start(bf16[32,48,2688]{2,1,0:T(8,128)(2,1)} %constant_dynamic-update-slice_fusion), calls=%async_computation.3 | async-start | bytes 16515072 | tf_op jit(solution)/shard_map/all_to_all | solution.py:216
  353.6 1.1 copy.34
  354.6 128.6 %all-to-all-done.3 = bf16[32,48,2688]{2,1,0:T(8,128)(2,1)} async-done(((bf16[32,48,2688]{2,1,0:T(8,128)(2,1)}), bf16[32,48,2688]{2,1,0:T(8,128)(2,1)}, u32[]{:S(2)}, u32[]{:S(2)}) %all-to-all-start.3) | async-done | bytes 8257568 | tf_op jit(solution)/shard_map/all_to_all | solution.py:216
  483.2 5.0 convert_reduce_fusion
  488.2 0.7 fusion.69
  489.1 6.7 %all-gather = bf16[4,6,80]{2,1,0:T(8,128)(2,1)S(1)} all-gather(bf16[1,6,80]{2,1,0:T(8,128)(2,1)S(1)} %reshape.702), channel_id=1, replica_groups=mesh['dp'=4,'ty'=4,'tx'=4,'tz'=2] {'dp'}, dimensions={0}, use_global_device_ids=true | all-gather | bytes 4800 | tf_op jit(solution)/shard_map/all_gather | solution.py:226
  495.8 0.8 convolution_convert_fusion.5
  (73 shorter events, 1.9 us)
Async XLA Ops:
  7.2 101.9 %copy-start = (bf16[128,2560]{1,0:T(8,128)(2,1)S(1)}, bf16[128,2560]{1,0:T(8,128)(2,1)}, u32[]{:S(2)}) copy-start(bf16[128,2560]{1,0:T(8,128)(2,1)} %param.24) | copy-start | bytes 1966084
  7.2 22.9 %copy-start.5 = (bf16[2560,64]{0,1:T(8,128)(2,1)S(1)}, bf16[2560,64]{0,1:T(8,128)(2,1)}, u32[]{:S(2)}) copy-start(bf16[2560,64]{0,1:T(8,128)(2,1)} %param.23) | copy-start | bytes 983044
  7.2 17.5 %copy-start.8 = (bf16[128]{0:T(256)(128)(2,1)S(1)}, bf16[128]{0:T(256)(128)(2,1)}, u32[]{:S(2)}) copy-start(bf16[128]{0:T(256)(128)(2,1)} %param.19) | copy-start | bytes 772
  7.2 17.5 %copy-start.9 = (bf16[128]{0:T(256)(128)(2,1)S(1)}, bf16[128]{0:T(256)(128)(2,1)}, u32[]{:S(2)}) copy-start(bf16[128]{0:T(256)(128)(2,1)} %param.20) | copy-start | bytes 772
  7.2 17.5 %copy-start.4 = (bf16[2560,128]{1,0:T(8,128)(2,1)S(1)}, bf16[2560,128]{1,0:T(8,128)(2,1)}, u32[]{:S(2)}) copy-start(bf16[2560,128]{1,0:T(8,128)(2,1)} %param.22) | copy-start | bytes 1966084
  7.2 87.2 %all-gather.4.cloned.1.call-start = ((), (), s32[]{:S(2)}) async-start(), calls=%async_computation.4 | async-start | bytes 8355840 | tf_op jit(solution)/shard_map/all_gather | solution.py:30
  20.3 9.8 %collective-permute-start = (bf16[2560,64]{0,1:T(8,128)(2,1)}, bf16[2560,64]{0,1:T(8,128)(2,1)S(1)}, u32[]{:S(2)}, u32[]{:S(2)}) collective-permute-start(bf16[2560,64]{0,1:T(8,128)(2,1)} %param.23), channel_id=1, source_target_pairs={{0,1},{1,0},{2,3},{3,2},{4,5},{5,4},{6,7},{7,6},{8,9},{9,8},{10,11... | collective-permute-start | bytes 983048 | tf_op jit(solution)/shard_map/ppermute | solution.py:19
  30.2 22.9 %collective-permute-start.1 = (bf16[2560,128]{0,1:T(8,128)(2,1)S(1)}, bf16[2560,128]{0,1:T(8,128)(2,1)S(1)}, u32[]{:S(2)}, u32[]{:S(2)}) collective-permute-start(bf16[2560,128]{0,1:T(8,128)(2,1)S(1)} %maximum_select_fusion.1), channel_id=1, source_target_pairs={{0,2},{1,3},{2,0},{3,1},{4,6},{5,7},{6,4},{7,5},{8,10},{9,11},{10,... | collective-permute-start | bytes 1966088 | tf_op jit(solution)/shard_map/ppermute | solution.py:19
  114.4 9.4 %copy-start.6 = (bf16[2560]{0:T(1024)(128)(2,1)S(1)}, bf16[2560]{0:T(1024)(128)(2,1)}, u32[]{:S(2)}) copy-start(bf16[2560]{0:T(1024)(128)(2,1)} %param.21) | copy-start | bytes 15364
  114.4 131.0 %all-to-all-start = ((bf16[32,48,2560]{2,1,0:T(8,128)(2,1)}), bf16[32,48,2560]{2,1,0:T(8,128)(2,1)}, u32[]{:S(2)}, u32[]{:S(2)}) async-start(bf16[32,48,2560]{2,1,0:T(8,128)(2,1)} %bitcast.123), calls=%async_computation | async-start | bytes 15728640 | tf_op jit(solution)/shard_map/all_to_all | solution.py:24
  123.7 202.4 %all-gather.6.cloned.1.call-start = ((), (), s32[]{:S(2)}) async-start(), calls=%async_computation.5 | async-start | bytes 8355840 | tf_op jit(solution)/shard_map/all_gather | solution.py:30
  123.8 126.1 %copy-start.2 = (bf16[48,2560]{1,0:T(8,128)(2,1)S(1)}, bf16[48,2560]{1,0:T(8,128)(2,1)}, u32[]{:S(2)}) copy-start(bf16[48,2560]{1,0:T(8,128)(2,1)} %param.14) | copy-start | bytes 737284
  250.0 8.6 %copy-start.10 = (s32[96]{0:T(128)S(1)}, s32[96]{0:T(128)}, u32[]{:S(2)}) copy-start(s32[96]{0:T(128)} %param.16) | copy-start | bytes 1156
  261.8 8.7 %all-to-all-start.1 = ((s32[4,1,24]{2,1,0:T(1,128)}), s32[4,1,24]{2,1,0:T(1,128)S(1)}, u32[]{:S(2)}, u32[]{:S(2)}) async-start(s32[4,1,24]{2,1,0:T(1,128)} %bitcast.29), calls=%async_computation.1 | async-start | bytes 4096 | tf_op jit(solution)/shard_map/all_to_all | solution.py:131
  272.1 54.0 %copy-start.7 = (bf16[2560,304]{0,1:T(8,128)(2,1)S(1)}, bf16[2560,304]{0,1:T(8,128)(2,1)}, u32[]{:S(2)}) copy-start(bf16[2560,304]{0,1:T(8,128)(2,1)} %param.26) | copy-start | bytes 4669444
  273.8 8.5 %all-to-all-start.2 = ((bf16[4,2,12288]{2,1,0:T(2,128)(2,1)}), bf16[4,2,12288]{2,1,0:T(2,128)(2,1)S(1)}, u32[]{:S(2)}, u32[]{:S(2)}) async-start(bf16[4,2,12288]{2,1,0:T(2,128)(2,1)} %reshape.716), calls=%async_computation.2 | async-start | bytes 393216 | tf_op jit(solution)/shard_map/all_to_all | solution.py:130
  334.0 1.4 copy-start.3
  344.4 138.8 %all-to-all-start.3 = ((bf16[32,48,2688]{2,1,0:T(8,128)(2,1)}), bf16[32,48,2688]{2,1,0:T(8,128)(2,1)}, u32[]{:S(2)}, u32[]{:S(2)}) async-start(bf16[32,48,2688]{2,1,0:T(8,128)(2,1)} %constant_dynamic-update-slice_fusion), calls=%async_computation.3 | async-start | bytes 16515072 | tf_op jit(solution)/shard_map/all_to_all | solution.py:216
  354.6 141.1 %copy-start.11 = (s32[16]{0:T(128)S(1)}, s32[16]{0:T(128)}, u32[]{:S(2)}) copy-start(s32[16]{0:T(128)} %param.17) | copy-start | bytes 196
  483.2 13.3 %copy-start.1 = (bf16[128,2560]{1,0:T(8,128)(2,1)S(1)}, bf16[128,2560]{1,0:T(8,128)(2,1)}, u32[]{:S(2)}) copy-start(bf16[128,2560]{1,0:T(8,128)(2,1)} %param.24) | copy-start | bytes 1966084
Sparse Core Ops, SparseCore 0:
  20.4 73.9 all-gather.3
  258.7 67.4 all-gather.5
where the time goes:
time: 504 us; the launch traced here: 503 us
  waiting for transfers between devices  365 us (72%)
  matrix products  32 us (6%)
  starting transfers between devices  31.4 us (6%)
  blocking collectives  24.9 us (5%)
  other arithmetic  22 us (4%)
  between operations  14.6 us (3%)
  local copies, waits for them, and re-layouts  13.6 us (3%)
    all_to_all x1, waiting for transfers between devices, per_device(): got = lax.all_to_all(payload, TENSOR, 0, 0, tiled=True)  129 us
    all_to_all x1, waiting for transfers between devices, scatter_sum(): got = lax.all_to_all(pieces, TENSOR, 0, 0, tiled=True)  122 us
    all_gather x2, waiting for transfers between devices, gather_rows(): return lax.all_gather(rows, ('ty', 'tx'), axis=0, tiled=True)  80.6 us
    ppermute x2, waiting for transfers between devices, partner_2(): return lax.ppermute(value, axis, pairs)  26.7 us
    all_gather x2, blocking collectives, gather_rows(): rows = lax.all_gather(rows, 'tz', axis=0, tiled=True)  18.2 us
  transfers between devices with their start and end apart: 8, of which 8 were waited for; matrix products, arithmetic and copies ran while one was open for 3% of the time, Pallas kernels for 0%

commit v1 on v0

--- a/solution.py
+++ b/solution.py
@@ -27,7 +27,17 @@
 
 def gather_rows(rows):
     rows = lax.all_gather(rows, "tz", axis=0, tiled=True)
-    return lax.all_gather(rows, ("ty", "tx"), axis=0, tiled=True)
+
+    def _produce_case(content, a_name, which_dim):
+        x_now = jnp.concatenate(
+            lax.all_to_all(
+                jnp.stack([content for _ in range(lax.axis_size(a_name))], axis=0), a_name, 0, 0
+            ),
+            axis=which_dim,
+        )
+        return x_now
+
+    return _produce_case(rows, ("ty", "tx"), 0)
 
 
 def row_norm(inputs, gain):

time: 504 us -> 612 us (1.21)
  waiting for transfers between devices: 365 us -> 452 us
  starting transfers between devices: 31.4 us -> 52.8 us
  between operations: 14.6 us -> 1.13 us
  local copies, waits for them, and re-layouts: 13.6 us -> 21.6 us
    all_to_all x0 -> x2, waiting for transfers between devices: none -> 105 us  [_produce_case(): lax.all_to_all(jnp.stack([content for _ in range(lax.axis_size(a_name))],...]
    ppermute x2, waiting for transfers between devices: 26.7 us -> 119 us  [partner_2(): return lax.ppermute(value, axis, pairs)]
    all_gather x2 -> x0, waiting for transfers between devices: 80.6 us -> none  [gather_rows(): return lax.all_gather(rows, ('ty', 'tx'), axis=0, tiled=True)]
    all_to_all x0 -> x2, starting transfers between devices: none -> 18.1 us  [_produce_case(): lax.all_to_all(jnp.stack([content for _ in range(lax.axis_size(a_name))],...]
    all_to_all x1, waiting for transfers between devices: 122 us -> 107 us  [scatter_sum(): got = lax.all_to_all(pieces, TENSOR, 0, 0, tiled=True)]
    another operation x0 -> x2, local copies, waits for them, and re-layouts: none -> 7.84 us  [_produce_case(): jnp.stack([content for _ in range(lax.axis_size(a_name))], axis=0)]
    all_to_all x1, waiting for transfers between devices: 129 us -> 121 us  [per_device(): got = lax.all_to_all(payload, TENSOR, 0, 0, tiled=True)]
  transfers between devices with their start and end apart: 8 -> 8, of which waited for: 8 -> 5; matrix products, arithmetic and copies ran while one was open for 3% -> 3% of each run, Pallas kernels for 0% -> 0%
where the time goes in v1:
time: 612 us; the launch traced here: 607 us
  waiting for transfers between devices  452 us (74%)
  starting transfers between devices  52.8 us (9%)
  matrix products  32 us (5%)
  blocking collectives  26.6 us (4%)
  local copies, waits for them, and re-layouts  21.6 us (4%)
  other arithmetic  20.7 us (3%)
    all_to_all x1, waiting for transfers between devices, per_device(): got = lax.all_to_all(payload, TENSOR, 0, 0, tiled=True)  121 us
    ppermute x2, waiting for transfers between devices, partner_2(): return lax.ppermute(value, axis, pairs)  119 us
    all_to_all x1, waiting for transfers between devices, scatter_sum(): got = lax.all_to_all(pieces, TENSOR, 0, 0, tiled=True)  107 us
    all_to_all x2, waiting for transfers between devices, _produce_case(): lax.all_to_all(jnp.stack([content for _ in range(lax.axis_size(a_name))],...  105 us
    all_gather x2, blocking collectives, gather_rows(): rows = lax.all_gather(rows, 'tz', axis=0, tiled=True)  19.6 us
    all_to_all x2, starting transfers between devices, _produce_case(): lax.all_to_all(jnp.stack([content for _ in range(lax.axis_size(a_name))],...  18.1 us
    all_to_all x1, starting transfers between devices, per_device(): got = lax.all_to_all(payload, TENSOR, 0, 0, tiled=True)  12.3 us
  transfers between devices with their start and end apart: 8, of which 5 were waited for; matrix products, arithmetic and copies ran while one was open for 3% of the time, Pallas kernels for 0%

profile of v1, /device:TPU:27, one launch (start us, length us, event | category | flops | bytes accessed | tf_op | source)
XLA Modules:
  0.0 606.6 jit_solution(11687497380582514720)
XLA Ops:
  0.6 0.8 convert_element_type.131
  1.4 1.1 fusion.62
  2.5 1.1 fusion.64
  3.6 9.9 %all_gather.9 = bf16[96,2560]{1,0:T(8,128)(2,1)S(1)} all-gather(bf16[48,2560]{1,0:T(8,128)(2,1)S(1)} %fusion.64), channel_id=1, replica_groups=mesh['dp'=4,'ty'=4,'tx'=4,'tz'=2] {'tz'}, dimensions={0}, use_global_device_ids=true | all-gather | bytes 737280 | tf_op jit(solution)/shard_map/all_gather | solution.py:29
  13.5 3.9 stack.12
  17.5 6.7 %all-to-all-start = ((bf16[16,96,2560]{2,1,0:T(8,128)(2,1)}), bf16[16,96,2560]{2,1,0:T(8,128)(2,1)}, u32[]{:S(2)}, u32[]{:S(2)}) async-start(bf16[16,96,2560]{2,1,0:T(8,128)(2,1)} %stack.12), calls=%async_computation | async-start | bytes 15728640 | tf_op jit(solution)/shard_map/all_to_all | solution.py:33
  24.2 2.8 collective-permute-start
  27.0 0.2 reduce-window.4
  27.3 1.1 copy.29
  28.4 4.9 collective-permute-done
  33.5 0.4 collective-permute-start.1
  33.9 114.3 %collective-permute-done.1 = bf16[2560,128]{0,1:T(8,128)(2,1)S(1)} collective-permute-done((bf16[2560,128]{0,1:T(8,128)(2,1)S(1)}, bf16[2560,128]{0,1:T(8,128)(2,1)S(1)}, u32[]{:S(2)}, u32[]{:S(2)}) %collective-permute-start.1) | collective-permute-done | bytes 655392 | tf_op jit(solution)/shard_map/ppermute | solution.py:19
  148.1 0.3 maximum_select_fusion
  148.4 5.7 fusion.129
  154.2 0.2 fusion.40
  154.5 0.1 fusion.42
  154.6 1.7 fusion.75
  156.4 0.7 select_reduce_fusion
  157.1 1.0 fusion.13
  158.1 1.1 fusion.32
  159.2 0.6 fusion.5
  159.8 0.9 fusion.20
  160.7 0.9 fusion.25
  161.7 0.4 select_reduce_fusion.1
  162.1 0.3 fusion.45
  162.4 0.6 fusion.24
  163.1 5.4 convolution_convert_fusion.1
  168.4 10.2 %all-to-all-start.1 = ((bf16[32,48,2560]{2,1,0:T(8,128)(2,1)}), bf16[32,48,2560]{2,1,0:T(8,128)(2,1)}, u32[]{:S(2)}, u32[]{:S(2)}) async-start(bf16[32,48,2560]{2,1,0:T(8,128)(2,1)} %bitcast.123), calls=%async_computation.1 | async-start | bytes 15728640 | tf_op jit(solution)/shard_map/all_to_all | solution.py:24
  178.8 0.1 reduce_window_sum.18
  178.9 0.2 select_reduce_fusion.2
  179.1 1.1 scatter_custom_fusion
  180.2 1.2 gather_fusion
  181.4 0.7 all_to_all.23
  182.1 0.2 fusion.90
  182.3 0.2 copy.31
  182.5 0.7 gather_fusion.1
  183.2 1.0 reshape.728
  184.2 106.8 %all-to-all-done.1 = bf16[32,48,2560]{2,1,0:T(8,128)(2,1)} async-done(((bf16[32,48,2560]{2,1,0:T(8,128)(2,1)}), bf16[32,48,2560]{2,1,0:T(8,128)(2,1)}, u32[]{:S(2)}, u32[]{:S(2)}) %all-to-all-start.1) | async-done | bytes 7864352 | tf_op jit(solution)/shard_map/all_to_all | solution.py:24
  291.0 5.6 all-to-all-start.2
  296.7 4.6 convert_reduce_fusion.1
  301.3 0.2 fusion.66
  301.5 3.4 all-to-all-start.3
  305.0 9.6 %all_gather.10 = bf16[96,2560]{1,0:T(8,128)(2,1)S(1)} all-gather(bf16[48,2560]{1,0:T(8,128)(2,1)S(1)} %fusion.68), channel_id=1, replica_groups=mesh['dp'=4,'ty'=4,'tx'=4,'tz'=2] {'tz'}, dimensions={0}, use_global_device_ids=true | all-gather | bytes 737280 | tf_op jit(solution)/shard_map/all_gather | solution.py:29
  314.7 3.9 stack.17
  318.6 11.4 %all-to-all-start.4 = ((bf16[16,96,2560]{2,1,0:T(8,128)(2,1)}), bf16[16,96,2560]{2,1,0:T(8,128)(2,1)}, u32[]{:S(2)}, u32[]{:S(2)}) async-start(bf16[16,96,2560]{2,1,0:T(8,128)(2,1)} %stack.17), calls=%async_computation.4 | async-start | bytes 15728640 | tf_op jit(solution)/shard_map/all_to_all | solution.py:33
  330.0 0.5 broadcast.489
  330.5 0.7 reduce.13
  331.3 0.3 reshape.729
  331.6 3.4 scatter_fusion
  335.1 0.2 convolution_convert_fusion.2
  335.5 105.1 %all-to-all-done.4 = bf16[16,96,2560]{2,1,0:T(8,128)(2,1)} async-done(((bf16[16,96,2560]{2,1,0:T(8,128)(2,1)}), bf16[16,96,2560]{2,1,0:T(8,128)(2,1)}, u32[]{:S(2)}, u32[]{:S(2)}) %all-to-all-start.4) | async-done | bytes 7864352 | tf_op jit(solution)/shard_map/all_to_all | solution.py:33
  440.6 7.8 %fusion.1 = f32[1536,608]{0,1:T(8,128)S(1)} fusion(bf16[1536,2560]{1,0:T(8,128)(2,1)} %bitcast.37, bf16[2560,304]{0,1:T(8,128)(2,1)S(1)} %copy-done.7, bf16[2560,304]{0,1:T(8,128)(2,1)} %param.25), kind=kOutput, calls=%fused_computation.12 | convolution fusion | flops 4787732480 | bytes 14712832 | tf_op jit(solution)/shard_map/dot_general | solution.py:194
  448.4 0.6 fusion.12
  449.0 0.8 copy-done.3
  449.8 6.8 %convolution_convert_fusion = bf16[1536,2688]{1,0:T(8,128)(2,1)} fusion(bf16[1536,304]{0,1:T(8,128)(2,1)S(1)} %fusion.12, bf16[304,2560]{1,0:T(8,128)(2,1)S(1)} %copy-done.3), kind=kOutput, calls=%fused_computation.6 | convolution fusion | flops 2514419712 | bytes 10747904 | tf_op jit(solution)/shard_map/dot_general | solution.py:220
  456.6 1.0 convolution_convert_fusion.3
  458.0 0.8 constant_dynamic-update-slice_fusion
  458.8 12.3 %all-to-all-start.5 = ((bf16[32,48,2688]{2,1,0:T(8,128)(2,1)}), bf16[32,48,2688]{2,1,0:T(8,128)(2,1)}, u32[]{:S(2)}, u32[]{:S(2)}) async-start(bf16[32,48,2688]{2,1,0:T(8,128)(2,1)} %constant_dynamic-update-slice_fusion), calls=%async_computation.5 | async-start | bytes 16515072 | tf_op jit(solution)/shard_map/all_to_all | solution.py:226
  471.1 1.1 copy.34
  472.1 120.8 %all-to-all-done.5 = bf16[32,48,2688]{2,1,0:T(8,128)(2,1)} async-done(((bf16[32,48,2688]{2,1,0:T(8,128)(2,1)}), bf16[32,48,2688]{2,1,0:T(8,128)(2,1)}, u32[]{:S(2)}, u32[]{:S(2)}) %all-to-all-start.5) | async-done | bytes 8257568 | tf_op jit(solution)/shard_map/all_to_all | solution.py:226
  592.9 5.0 convert_reduce_fusion
  597.8 0.7 fusion.69
  598.8 7.0 %all-gather = bf16[4,6,80]{2,1,0:T(8,128)(2,1)S(1)} all-gather(bf16[1,6,80]{2,1,0:T(8,128)(2,1)S(1)} %reshape.714), channel_id=1, replica_groups=mesh['dp'=4,'ty'=4,'tx'=4,'tz'=2] {'dp'}, dimensions={0}, use_global_device_ids=true | all-gather | bytes 4800 | tf_op jit(solution)/shard_map/all_gather | solution.py:236
  605.8 0.8 convolution_convert_fusion.5
  (75 shorter events, 1.8 us)
Async XLA Ops:
  0.6 162.4 %copy-start = (bf16[128,2560]{1,0:T(8,128)(2,1)S(1)}, bf16[128,2560]{1,0:T(8,128)(2,1)}, u32[]{:S(2)}) copy-start(bf16[128,2560]{1,0:T(8,128)(2,1)} %param.24) | copy-start | bytes 1966084
  17.4 6.8 %copy-start.5 = (bf16[2560,64]{0,1:T(8,128)(2,1)S(1)}, bf16[2560,64]{0,1:T(8,128)(2,1)}, u32[]{:S(2)}) copy-start(bf16[2560,64]{0,1:T(8,128)(2,1)} %param.23) | copy-start | bytes 983044
  17.4 9.5 %copy-start.8 = (s32[1,6]{1,0:T(1,128)S(1)}, s32[1,6]{1,0:T(1,128)}, u32[]{:S(2)}) copy-start(s32[1,6]{1,0:T(1,128)} %param.15) | copy-start | bytes 76
  17.4 9.9 %copy-start.4 = (bf16[2560,128]{1,0:T(8,128)(2,1)S(1)}, bf16[2560,128]{1,0:T(8,128)(2,1)}, u32[]{:S(2)}) copy-start(bf16[2560,128]{1,0:T(8,128)(2,1)} %param.22) | copy-start | bytes 1966084
  17.4 10.9 %copy-start.9 = (bf16[128]{0:T(256)(128)(2,1)S(1)}, bf16[128]{0:T(256)(128)(2,1)}, u32[]{:S(2)}) copy-start(bf16[128]{0:T(256)(128)(2,1)} %param.19) | copy-start | bytes 772
  17.4 10.9 %copy-start.10 = (bf16[128]{0:T(256)(128)(2,1)S(1)}, bf16[128]{0:T(256)(128)(2,1)}, u32[]{:S(2)}) copy-start(bf16[128]{0:T(256)(128)(2,1)} %param.20) | copy-start | bytes 772
  17.5 130.9 %all-to-all-start = ((bf16[16,96,2560]{2,1,0:T(8,128)(2,1)}), bf16[16,96,2560]{2,1,0:T(8,128)(2,1)}, u32[]{:S(2)}, u32[]{:S(2)}) async-start(bf16[16,96,2560]{2,1,0:T(8,128)(2,1)} %stack.12), calls=%async_computation | async-start | bytes 15728640 | tf_op jit(solution)/shard_map/all_to_all | solution.py:33
  24.2 9.1 %collective-permute-start = (bf16[2560,64]{0,1:T(8,128)(2,1)S(1)}, bf16[2560,64]{0,1:T(8,128)(2,1)S(1)}, u32[]{:S(2)}, u32[]{:S(2)}) collective-permute-start(bf16[2560,64]{0,1:T(8,128)(2,1)S(1)} %copy-done.5), channel_id=1, source_target_pairs={{0,1},{1,0},{2,3},{3,2},{4,5},{5,4},{6,7},{7,6},{8,9},{9,8},{10,11... | collective-permute-start | bytes 983048 | tf_op jit(solution)/shard_map/ppermute | solution.py:19
  33.5 114.7 %collective-permute-start.1 = (bf16[2560,128]{0,1:T(8,128)(2,1)S(1)}, bf16[2560,128]{0,1:T(8,128)(2,1)S(1)}, u32[]{:S(2)}, u32[]{:S(2)}) collective-permute-start(bf16[2560,128]{0,1:T(8,128)(2,1)S(1)} %maximum_select_fusion.1), channel_id=1, source_target_pairs={{0,2},{1,3},{2,0},{3,1},{4,6},{5,7},{6,4},{7,5},{8,10},{9,11},{10,... | collective-permute-start | bytes 1966088 | tf_op jit(solution)/shard_map/ppermute | solution.py:19
  168.4 10.2 %copy-start.11 = (s32[96]{0:T(128)S(1)}, s32[96]{0:T(128)}, u32[]{:S(2)}) copy-start(s32[96]{0:T(128)} %param.16) | copy-start | bytes 1156
  168.4 13.7 %copy-start.6 = (bf16[2560]{0:T(1024)(128)(2,1)S(1)}, bf16[2560]{0:T(1024)(128)(2,1)}, u32[]{:S(2)}) copy-start(bf16[2560]{0:T(1024)(128)(2,1)} %param.21) | copy-start | bytes 15364
  168.4 122.6 %all-to-all-start.1 = ((bf16[32,48,2560]{2,1,0:T(8,128)(2,1)}), bf16[32,48,2560]{2,1,0:T(8,128)(2,1)}, u32[]{:S(2)}, u32[]{:S(2)}) async-start(bf16[32,48,2560]{2,1,0:T(8,128)(2,1)} %bitcast.123), calls=%async_computation.1 | async-start | bytes 15728640 | tf_op jit(solution)/shard_map/all_to_all | solution.py:24
  291.0 10.4 %all-to-all-start.2 = ((s32[4,1,24]{2,1,0:T(1,128)}), s32[4,1,24]{2,1,0:T(1,128)S(1)}, u32[]{:S(2)}, u32[]{:S(2)}) async-start(s32[4,1,24]{2,1,0:T(1,128)} %bitcast.30), calls=%async_computation.2 | async-start | bytes 4096 | tf_op jit(solution)/shard_map/all_to_all | solution.py:141
  296.7 4.6 copy-start.2
  301.5 13.2 %all-to-all-start.3 = ((bf16[4,2,12288]{2,1,0:T(2,128)(2,1)}), bf16[4,2,12288]{2,1,0:T(2,128)(2,1)S(1)}, u32[]{:S(2)}, u32[]{:S(2)}) async-start(bf16[4,2,12288]{2,1,0:T(2,128)(2,1)} %reshape.728), calls=%async_computation.3 | async-start | bytes 393216 | tf_op jit(solution)/shard_map/all_to_all | solution.py:140
  318.6 122.0 %all-to-all-start.4 = ((bf16[16,96,2560]{2,1,0:T(8,128)(2,1)}), bf16[16,96,2560]{2,1,0:T(8,128)(2,1)}, u32[]{:S(2)}, u32[]{:S(2)}) async-start(bf16[16,96,2560]{2,1,0:T(8,128)(2,1)} %stack.17), calls=%async_computation.4 | async-start | bytes 15728640 | tf_op jit(solution)/shard_map/all_to_all | solution.py:33
  330.0 110.6 %copy-start.7 = (bf16[2560,304]{0,1:T(8,128)(2,1)S(1)}, bf16[2560,304]{0,1:T(8,128)(2,1)}, u32[]{:S(2)}) copy-start(bf16[2560,304]{0,1:T(8,128)(2,1)} %param.26) | copy-start | bytes 4669444
  448.4 1.4 copy-start.3
  458.8 134.1 %all-to-all-start.5 = ((bf16[32,48,2688]{2,1,0:T(8,128)(2,1)}), bf16[32,48,2688]{2,1,0:T(8,128)(2,1)}, u32[]{:S(2)}, u32[]{:S(2)}) async-start(bf16[32,48,2688]{2,1,0:T(8,128)(2,1)} %constant_dynamic-update-slice_fusion), calls=%async_computation.5 | async-start | bytes 16515072 | tf_op jit(solution)/shard_map/all_to_all | solution.py:226
  472.1 133.7 %copy-start.12 = (s32[16]{0:T(128)S(1)}, s32[16]{0:T(128)}, u32[]{:S(2)}) copy-start(s32[16]{0:T(128)} %param.17) | copy-start | bytes 196
  592.9 13.7 %copy-start.1 = (bf16[128,2560]{1,0:T(8,128)(2,1)S(1)}, bf16[128,2560]{1,0:T(8,128)(2,1)}, u32[]{:S(2)}) copy-start(bf16[128,2560]{1,0:T(8,128)(2,1)} %param.24) | copy-start | bytes 1966084
